TPU v7x, 32 devices: a whole 2x2x4 slice. The times are simulated.
32 devices in a mesh: shard: 4 (over z), rep: 8 (over y, x, core).
Axes of the slice: x: 2, y: 2, z: 4, core: 2. Of those that a mesh axis runs over, the one named last changes fastest.
Arguments:
- grads: bfloat16 [1, 8192, 28672], P(None, 'shard', 'rep'), may hold values from -81 to 81
- seeds: int32 [1], replicated, may hold values from 0 to 999999
Outputs:
- projected: bfloat16 [512, 1, 28672], P('shard', None, 'rep')
All inputs are finite; a program needn't handle non-finite values.
Results may differ from a plain program's by a relative error of at most 0.0056.
Values may be sent and summed in bfloat16 or wider, within the bound.
No kernel may reach another device: no remote copies, remote signals or barrier semaphores. Data moves between devices by JAX's collectives and lax.ppermute only.
A program may use at most 128 MiB of HBM per device.

v0:
```python
import jax
import jax.numpy as jnp
from jax import lax
from jax.sharding import PartitionSpec as P

RANK = 512
mix_first = 668265263
mix_second = -2048144789
mix_third = -1028477387


def sketch_table(seeds, first_row, count, rank):
    rows = first_row + lax.iota(jnp.int32, count)
    columns = lax.iota(jnp.int32, rank)
    counter = rows[:, None] * jnp.int32(rank) + columns[None, :]
    hashed = jnp.bitwise_xor(counter[None, :, :], (seeds * jnp.int32(mix_first))[:, None, None])
    hashed = hashed * jnp.int32(mix_second)
    hashed = jnp.bitwise_xor(hashed, lax.shift_right_logical(hashed, jnp.int32(15)))
    hashed = hashed * jnp.int32(mix_third)
    hashed = jnp.bitwise_xor(hashed, lax.shift_right_logical(hashed, jnp.int32(13)))
    unit = lax.shift_right_logical(hashed, jnp.int32(8)).astype(jnp.float32) * (1.0 / 16777216.0)
    return (2.0 * unit - 1.0).astype(jnp.bfloat16)


def body(grads, seeds):
    mats, depth, width = grads.shape
    rows_whole = lax.all_to_all(grads, "rep", split_axis=1, concat_axis=2, tiled=True)
    block = rows_whole.shape[2] // 8

    def add_block(step, total):
        start = step * block
        table = sketch_table(seeds, start, block, RANK)
        piece = lax.dynamic_slice_in_dim(rows_whole, start, block, 2)
        return total + jnp.einsum("mdc,mcr->dmr", piece, table, preferred_element_type=jnp.float32)

    sketch_rows = lax.fori_loop(
        0, 8, add_block, jnp.zeros((rows_whole.shape[1], mats, RANK), jnp.float32)
    )
    local_gram = jnp.einsum(
        "dmr,dms->mrs",
        sketch_rows,
        sketch_rows,
        precision=lax.Precision.HIGHEST,
        preferred_element_type=jnp.float32,
    )
    gram = lax.psum(local_gram, ("shard", "rep"))
    factor = jnp.linalg.cholesky(gram)
    own_rows = jnp.transpose(sketch_rows, (1, 0, 2))
    basis_rows = lax.linalg.triangular_solve(
        factor, own_rows, left_side=False, lower=True, transpose_a=True
    ).astype(jnp.bfloat16)
    partial_sum = jnp.einsum(
        "mdr,mdc->rmc",
        lax.all_gather(basis_rows, "rep", axis=1, tiled=True),
        grads,
        preferred_element_type=jnp.float32,
    )
    projected = lax.psum_scatter(partial_sum, "shard", scatter_dimension=0, tiled=True)
    return projected.astype(jnp.bfloat16)


def solution(mesh):
    return jax.shard_map(
        body,
        mesh=mesh,
        in_specs=(P(None, "shard", "rep"), P()),
        out_specs=P("shard", None, "rep"),
        check_vma=False,
    )
```

profile of v0, /device:TPU:0, one launch (start us, length us, event | category | flops | bytes accessed | tf_op | source)
XLA Modules:
  0.0 861.6 jit_solution(14677463218900408071)
XLA Ops:
  6.5 26.0 %copy.30 = bf16[1,2048,3584]{2,0,1:T(2,128)(2,1)} copy(bf16[1,2048,3584]{2,1,0:T(8,128)(2,1)} %param.4) | data formatting | bytes 29360128 | tf_op args[0]
  32.6 0.5 broadcast.502
  33.1 94.1 %reduce.36 = bf16[2048,3584]{1,0:T(8,128)(2,1)} reduce(bf16[2048,1,3584]{2,1,0:T(2,128)(2,1)} %bitcast.210, bf16[]{:T(256)} %broadcast.502), dimensions={1}, to_apply=%bitcast.195.reduce_sub_computation | reduce | bytes 29360130
  127.2 16.3 %reshape.459 = bf16[8,2,458752]{2,1,0:T(2,128)(2,1)} reshape(bf16[2048,3584]{1,0:T(8,128)(2,1)} %reduce.36) | data formatting | bytes 29360128
  143.5 5.6 all-to-all-start
  149.1 0.2 all-reduce.3.cloned.1.call-start
  149.9 161.3 %all-to-all-done = bf16[8,2,458752]{2,1,0:T(2,128)(2,1)} async-done(((bf16[8,2,458752]{2,1,0:T(2,128)(2,1)}), bf16[8,2,458752]{2,1,0:T(2,128)(2,1)}, u32[]{:S(2)}, u32[]{:S(2)}) %all-to-all-start) | async-done | bytes 14680096 | tf_op jit(solution)/shard_map/all_to_all | solution.py:27
  311.2 20.2 %reshape.460 = bf16[2048,1,3584]{2,1,0:T(2,128)(2,1)} reshape(bf16[8,2,458752]{2,1,0:T(2,128)(2,1)} %all-to-all-done) | data formatting | bytes 29360128
  331.4 19.4 %copy.28 = bf16[1,2048,3584]{2,1,0:T(8,128)(2,1)} copy(bf16[1,2048,3584]{2,0,1:T(2,128)(2,1)} %bitcast.211) | data formatting | bytes 29360128
  350.8 18.7 %copy.21 = bf16[1,256,8,3584]{1,3,2,0:T(8,128)(2,1)} copy(bf16[1,256,8,3584]{3,1,2,0:T(8,128)(2,1)} %bitcast.212) | data formatting | bytes 29360128 | tf_op jit(solution)/shard_map/all_to_all | solution.py:27
  369.5 42.8 %while.18 = (s32[]{:T(128)}, f32[256,1,512]{0,2,1:T(8,128)S(1)}, s32[1]{0:T(128)}, bf16[1,256,28672]{1,2,0:T(8,128)(2,1)}, s32[]{:T(128)}, /*index=5*/s32[]{:T(128)}, s32[]{:T(128)}, s32[]{:T(128)}) while((s32[]{:T(128)}, f32[256,1,512]{0,2,1:T(8,128)S(1)}, s32[1]{0:T(128)}, bf16[1,256,28672]{1,2,0:T(8,128)(2,1)}, s32[]{:T(128)}, ...), condition=%wide.region_1.0_spmd.clone, body=%wide.region_0.0_spmd.clone.sunk | while | flops 963648512 | bytes 2912917 | solution.py:36
  369.5 5.3 fusion.77
  374.8 5.3 fusion.77
  380.2 5.3 fusion.77
  385.5 5.3 fusion.77
  390.9 5.3 fusion.77
  396.2 5.3 fusion.77
  401.6 5.3 fusion.77
  407.0 5.3 fusion.77
  412.3 2.1 convolution_bitcast_fusion
  414.4 0.3 all-gather.2.cloned.1.call-start
  414.7 0.2 copy.23
  414.9 130.6 %all-reduce.3.cloned.1.call-done = f32[1,512,512]{1,2,0:T(8,128)} async-done(((f32[1,512,512]{1,2,0:T(8,128)}), f32[1,512,512]{1,2,0:T(8,128)}) %all-reduce.3.cloned.1.call-update) | async-done | bytes 1048592 | tf_op jit(solution)/shard_map/psum | solution.py:46
  545.5 1.6 copy.25
  547.1 1.4 fusion.47
  548.5 11.7 %custom-call.34 = f32[1,128,128]{2,1,0:T(8,128)S(1)} custom-call(f32[1,128,128]{2,1,0:T(8,128)S(1)} %cholesky.267), custom_call_target="Cholesky" | custom-call | tf_op jit(solution)/shard_map/jit(cholesky)/cholesky | solution.py:47
  560.3 9.8 %custom-call.35 = f32[1,1,128,128]{2,3,1,0:T(8,128)S(1)} custom-call(f32[1,1,128,128]{3,2,1,0:T(8,128)S(1)} %get-tuple-element.173), custom_call_target="InvertDiagBlocksLowerTriangular" | custom-call | tf_op jit(solution)/shard_map/jit(cholesky)/cholesky | solution.py:47
  570.2 0.3 constant_dynamic-update-slice_fusion.3
  570.5 0.3 fusion.35
  570.9 11.7 %custom-call.36 = f32[1,128,128]{2,1,0:T(8,128)S(1)} custom-call(f32[1,128,128]{2,1,0:T(8,128)S(1)} %cholesky.271), custom_call_target="Cholesky" | custom-call | tf_op jit(solution)/shard_map/jit(cholesky)/cholesky | solution.py:47
  582.6 10.2 %custom-call.37 = f32[1,1,128,128]{2,3,1,0:T(8,128)S(1)} custom-call(f32[1,1,128,128]{3,2,1,0:T(8,128)S(1)} %get-tuple-element.170), custom_call_target="InvertDiagBlocksLowerTriangular" | custom-call | tf_op jit(solution)/shard_map/jit(cholesky)/cholesky | solution.py:47
  592.8 0.3 fusion.36
  593.1 0.4 fusion.39
  593.5 11.7 %custom-call.38 = f32[1,128,128]{2,1,0:T(8,128)S(1)} custom-call(f32[1,128,128]{2,1,0:T(8,128)S(1)} %cholesky.276), custom_call_target="Cholesky" | custom-call | tf_op jit(solution)/shard_map/jit(cholesky)/cholesky | solution.py:47
  605.2 0.7 compare_reduce_fusion.1
  606.0 9.8 %custom-call.39 = f32[1,1,128,128]{2,3,1,0:T(8,128)S(1)} custom-call(f32[1,1,128,128]{3,2,1,0:T(8,128)S(1)} %get-tuple-element.167), custom_call_target="InvertDiagBlocksLowerTriangular" | custom-call | tf_op jit(solution)/shard_map/jit(cholesky)/cholesky | solution.py:47
  615.8 0.2 fusion.45
  616.0 0.4 fusion.46
  616.4 11.7 %custom-call.40 = f32[1,128,128]{2,1,0:T(8,128)S(1)} custom-call(f32[1,128,128]{2,1,0:T(8,128)S(1)} %fusion.46), custom_call_target="Cholesky" | custom-call | tf_op jit(solution)/shard_map/jit(cholesky)/cholesky | solution.py:47
  628.1 0.6 compare_reduce_fusion
  628.8 0.9 compare_reduce_fusion.2
  632.1 0.1 select_select_fusion
  632.3 8.1 while.17
  632.4 0.6 fusion.74
  633.0 1.3 bitcast_dynamic-update-slice_fusion.2
  634.4 0.6 fusion.74
  635.0 1.3 bitcast_dynamic-update-slice_fusion.2
  636.5 0.6 fusion.74
  637.1 1.3 bitcast_dynamic-update-slice_fusion.2
  638.5 0.6 fusion.74
  639.1 1.3 bitcast_dynamic-update-slice_fusion.2
  640.4 39.3 %custom-call.41 = f32[1,4,128,128]{2,3,1,0:T(8,128)S(1)} custom-call(f32[1,4,128,128]{3,2,1,0:T(8,128)S(1)} %bitcast.221), custom_call_target="InvertDiagBlocksLowerTriangular" | custom-call | tf_op jit(solution)/shard_map/triangular_solve | solution.py:49
  679.8 0.3 bitcast_convert_fusion
  680.1 0.4 fusion.38
  680.5 0.3 fusion.64
  680.8 0.6 fusion.41
  681.4 0.3 fusion.63
  681.7 0.8 fusion.43
  682.6 0.3 fusion.44
  682.9 0.7 pad_maximum_fusion
  683.7 27.2 %all-gather.2.cloned.1.call-done = bf16[1,2048,512]{1,2,0:T(8,128)(2,1)} async-done(((bf16[1,256,512]{1,2,0:T(8,128)(2,1)}), bf16[1,2048,512]{1,2,0:T(8,128)(2,1)}) %all-gather.2.cloned.1.call-update) | async-done | bytes 2097168 | tf_op jit(solution)/shard_map/all_gather | solution.py:54
  710.9 13.5 %fusion.31 = f32[512,1,3584]{2,0,1:T(8,128)} fusion(bf16[1,2048,3584]{2,1,0:T(8,128)(2,1)} %param.4, bf16[1,2048,512]{1,2,0:T(8,128)(2,1)} %all-gather.2.cloned.1.call-done), kind=kOutput, calls=%fused_computation.27 | convolution fusion | flops 7516192768 | bytes 24117248 | tf_op jit(solution)/shard_map/mdr,mdc->rmc/dot_general | solution.py:52
  724.4 127.9 %reduce-scatter.2.cloned.1.call-done = f32[128,1,3584]{2,0,1:T(8,128)} async-done(((f32[512,1,3584]{2,0,1:T(8,128)}), f32[128,1,3584]{2,0,1:T(8,128)}) %reduce-scatter.2.cloned.1.call-update) | async-done | bytes 1835024 | tf_op jit(solution)/shard_map/reduce_scatter | solution.py:58
  852.3 2.5 convert_element_type.66
  (28 shorter events, 0.7 us)
Async XLA Ops:
  143.5 167.7 %all-to-all-start = ((bf16[8,2,458752]{2,1,0:T(2,128)(2,1)}), bf16[8,2,458752]{2,1,0:T(2,128)(2,1)}, u32[]{:S(2)}, u32[]{:S(2)}) async-start(bf16[8,2,458752]{2,1,0:T(2,128)(2,1)} %reshape.459), calls=%async_computation | async-start | bytes 29360128 | tf_op jit(solution)/shard_map/all_to_all | solution.py:27
  149.1 396.4 %all-reduce.3.cloned.1.call-start = ((), (), s32[]{:S(2)}) async-start(), calls=%async_computation.2 | async-start | bytes 2097152 | tf_op jit(solution)/shard_map/psum | solution.py:46
  414.4 296.5 %all-gather.2.cloned.1.call-start = ((), (), s32[]{:S(2)}) async-start(), calls=%async_computation.3 | async-start | bytes 2359296 | tf_op jit(solution)/shard_map/all_gather | solution.py:54
  683.6 168.7 %reduce-scatter.2.cloned.1.call-start = ((), (), s32[]{:S(2)}) async-start(), calls=%async_computation.4 | async-start | bytes 9175040 | tf_op jit(solution)/shard_map/reduce_scatter | solution.py:58
Sparse Core Ops, SparseCore 0:
  414.5 130.9 all-reduce.2
  683.8 27.0 all-gather.1
  724.5 127.7 reduce-scatter.1
where the time goes:
time: 869 us; the launch traced here: 862 us
  waiting for transfers between devices  447 us (51%)
  other arithmetic  217 us (25%)
  local copies, waits for them, and re-layouts  111 us (13%)
  matrix products  63 us (7%)
  between operations  16.7 us (2%)
    all_to_all x1, waiting for transfers between devices, body(): lax.all_to_all(grads, 'rep', split_axis=1, concat_axis=2, tiled=True)  161 us
    psum x1, waiting for transfers between devices, body(): gram = lax.psum(local_gram, ('shard', 'rep'))  131 us
    reduce_scatter x1, waiting for transfers between devices, body(): lax.psum_scatter(partial_sum, 'shard', scatter_dimension=0, tiled=True)  128 us
    unnamed x3, other arithmetic  94.1 us
    unnamed x5, local copies, waits for them, and re-layouts  82.4 us
    another operation x14, other arithmetic, body(): factor = jnp.linalg.cholesky(gram)  79 us
    dot_general x8, matrix products, add_block(): jnp.einsum('mdc,mcr->dmr', piece, table, preferred_element_type=jnp.float32)  42.5 us
    another operation x4, other arithmetic, body(): lax.linalg.triangular_solve(factor, own_rows, left_side=False, lower=True...  40.2 us
  transfers between devices with their start and end apart: 4, of which 4 were waited for; matrix products, arithmetic and copies ran while one was open for 0% of the time, Pallas kernels for 0%

commit v1 on v0

--- a/solution.py
+++ b/solution.py
@@ -24,7 +24,12 @@
 
 def body(grads, seeds):
     mats, depth, width = grads.shape
-    rows_whole = lax.all_to_all(grads, "rep", split_axis=1, concat_axis=2, tiled=True)
+    rows_whole = jnp.concatenate(
+        jax.lax.all_to_all(
+            jnp.stack(jnp.split(grads, jax.lax.axis_size("rep"), 1), 0), "rep", 0, 0
+        ),
+        2,
+    )
     block = rows_whole.shape[2] // 8
 
     def add_block(step, total):

time: 869 us -> 709 us (0.82)
  other arithmetic: 217 us -> 123 us
  local copies, waits for them, and re-layouts: 111 us -> 46.6 us
    unnamed x3 -> x2, other arithmetic: 94.1 us -> 0.01 us
    unnamed x5 -> x7, local copies, waits for them, and re-layouts: 82.4 us -> 20.2 us
    all_to_all x1 -> x0, local copies, waits for them, and re-layouts: 18.7 us -> none  [body(): lax.all_to_all(grads, 'rep', split_axis=1, concat_axis=2, tiled=True)]
    reshape x0 -> x1, local copies, waits for them, and re-layouts: none -> 13.7 us  [body(): jnp.concatenate(jax.lax.all_to_all(jnp.stack(jnp.split(grads, jax.lax.axi...]
where the time goes in v1:
time: 709 us; the launch traced here: 703 us
  waiting for transfers between devices  447 us (63%)
  other arithmetic  123 us (17%)
  matrix products  63.1 us (9%)
  local copies, waits for them, and re-layouts  46.6 us (7%)
  between operations  16.8 us (2%)
    all_to_all x1, waiting for transfers between devices, body(): jax.lax.all_to_all(jnp.stack(jnp.split(grads, jax.lax.axis_size('rep'), 1...  161 us
    psum x1, waiting for transfers between devices, body(): gram = lax.psum(local_gram, ('shard', 'rep'))  130 us
    reduce_scatter x1, waiting for transfers between devices, body(): lax.psum_scatter(partial_sum, 'shard', scatter_dimension=0, tiled=True)  128 us
    another operation x14, other arithmetic, body(): factor = jnp.linalg.cholesky(gram)  78.8 us
    dot_general x8, matrix products, add_block(): jnp.einsum('mdc,mcr->dmr', piece, table, preferred_element_type=jnp.float32)  42.5 us
    another operation x4, other arithmetic, body(): lax.linalg.triangular_solve(factor, own_rows, left_side=False, lower=True...  40.2 us
    all_gather x1, waiting for transfers between devices, body(): lax.all_gather(basis_rows, 'rep', axis=1, tiled=True)  27.2 us
    unnamed x7, local copies, waits for them, and re-layouts  20.2 us
  transfers between devices with their start and end apart: 4, of which 4 were waited for; matrix products, arithmetic and copies ran while one was open for 0% of the time, Pallas kernels for 0%

profile of v1, /device:TPU:0, one launch (start us, length us, event | category | flops | bytes accessed | tf_op | source)
XLA Modules:
  0.0 702.9 jit_solution(16570029235851708633)
XLA Ops:
  6.5 2.9 bitcast_dynamic-update-slice_fusion.8
  9.4 2.8 bitcast_dynamic-update-slice_fusion.7
  12.2 2.9 bitcast_dynamic-update-slice_fusion.6
  15.1 2.9 bitcast_dynamic-update-slice_fusion.5
  18.0 2.9 bitcast_dynamic-update-slice_fusion.4
  21.0 2.9 bitcast_dynamic-update-slice_fusion.3
  23.8 2.9 bitcast_dynamic-update-slice_fusion.2
  26.7 2.9 bitcast_dynamic-update-slice_fusion.1
  29.6 5.5 all-to-all-start
  35.8 161.4 %all-to-all-done = bf16[8,1,256,3584]{3,2,1,0:T(8,128)(2,1)} async-done(((bf16[8,1,256,3584]{3,2,1,0:T(8,128)(2,1)}), bf16[8,1,256,3584]{3,2,1,0:T(8,128)(2,1)}, u32[]{:S(2)}, u32[]{:S(2)}) %all-to-all-start) | async-done | bytes 14680096 | tf_op jit(solution)/shard_map/all_to_all | solution.py:28
  197.3 13.7 %copy.12 = bf16[8,1,32,8,3584]{4,3,0,2,1:T(8,128)(2,1)} copy(bf16[8,1,32,8,3584]{4,3,2,1,0:T(8,128)(2,1)} %bitcast.69) | data formatting | bytes 29360128 | tf_op jit(solution)/shard_map/reshape | solution.py:27
  210.9 42.8 %while.18 = (s32[]{:T(128)}, f32[256,1,512]{0,2,1:T(8,128)S(1)}, s32[1]{0:T(128)}, bf16[1,256,28672]{2,1,0:T(8,128)(2,1)}, s32[]{:T(128)}, /*index=5*/s32[]{:T(128)}, s32[]{:T(128)}, s32[]{:T(128)}) while((s32[]{:T(128)}, f32[256,1,512]{0,2,1:T(8,128)S(1)}, s32[1]{0:T(128)}, bf16[1,256,28672]{2,1,0:T(8,128)(2,1)}, s32[]{:T(128)}, ...), condition=%wide.region_1.0_spmd.clone, body=%wide.region_0.0_spmd.clone.sunk | while | flops 963648512 | bytes 2912917 | solution.py:41
  210.9 5.3 fusion.77
  216.3 5.3 fusion.77
  221.6 5.3 fusion.77
  227.0 5.3 fusion.77
  232.3 5.3 fusion.77
  237.7 5.3 fusion.77
  243.1 5.3 fusion.77
  248.4 5.3 fusion.77
  253.7 2.1 convolution_bitcast_fusion
  255.8 0.5 all-gather.2.cloned.1.call-start
  256.4 0.2 copy.8
  256.6 130.4 %all-reduce.3.cloned.1.call-done = f32[1,512,512]{1,2,0:T(8,128)} async-done(((f32[1,512,512]{1,2,0:T(8,128)}), f32[1,512,512]{1,2,0:T(8,128)}) %all-reduce.3.cloned.1.call-update) | async-done | bytes 1048592 | tf_op jit(solution)/shard_map/psum | solution.py:51
  387.0 1.6 copy.10
  388.5 1.4 fusion.47
  390.0 11.7 %custom-call.34 = f32[1,128,128]{2,1,0:T(8,128)S(1)} custom-call(f32[1,128,128]{2,1,0:T(8,128)S(1)} %cholesky.267), custom_call_target="Cholesky" | custom-call | tf_op jit(solution)/shard_map/jit(cholesky)/cholesky | solution.py:52
  401.7 9.8 %custom-call.35 = f32[1,1,128,128]{2,3,1,0:T(8,128)S(1)} custom-call(f32[1,1,128,128]{3,2,1,0:T(8,128)S(1)} %get-tuple-element.169), custom_call_target="InvertDiagBlocksLowerTriangular" | custom-call | tf_op jit(solution)/shard_map/jit(cholesky)/cholesky | solution.py:52
  411.7 0.3 constant_dynamic-update-slice_fusion.3
  412.0 0.3 fusion.35
  412.4 11.7 %custom-call.36 = f32[1,128,128]{2,1,0:T(8,128)S(1)} custom-call(f32[1,128,128]{2,1,0:T(8,128)S(1)} %cholesky.271), custom_call_target="Cholesky" | custom-call | tf_op jit(solution)/shard_map/jit(cholesky)/cholesky | solution.py:52
  424.1 10.0 %custom-call.37 = f32[1,1,128,128]{2,3,1,0:T(8,128)S(1)} custom-call(f32[1,1,128,128]{3,2,1,0:T(8,128)S(1)} %get-tuple-element.166), custom_call_target="InvertDiagBlocksLowerTriangular" | custom-call | tf_op jit(solution)/shard_map/jit(cholesky)/cholesky | solution.py:52
  434.1 0.3 fusion.36
  434.3 0.4 fusion.39
  434.7 11.7 %custom-call.38 = f32[1,128,128]{2,1,0:T(8,128)S(1)} custom-call(f32[1,128,128]{2,1,0:T(8,128)S(1)} %cholesky.276), custom_call_target="Cholesky" | custom-call | tf_op jit(solution)/shard_map/jit(cholesky)/cholesky | solution.py:52
  446.5 0.7 compare_reduce_fusion.1
  447.2 9.8 %custom-call.39 = f32[1,1,128,128]{2,3,1,0:T(8,128)S(1)} custom-call(f32[1,1,128,128]{3,2,1,0:T(8,128)S(1)} %get-tuple-element.163), custom_call_target="InvertDiagBlocksLowerTriangular" | custom-call | tf_op jit(solution)/shard_map/jit(cholesky)/cholesky | solution.py:52
  457.0 0.2 fusion.45
  457.2 0.4 fusion.46
  457.6 11.7 %custom-call.40 = f32[1,128,128]{2,1,0:T(8,128)S(1)} custom-call(f32[1,128,128]{2,1,0:T(8,128)S(1)} %fusion.46), custom_call_target="Cholesky" | custom-call | tf_op jit(solution)/shard_map/jit(cholesky)/cholesky | solution.py:52
  469.4 0.6 compare_reduce_fusion
  470.0 0.9 compare_reduce_fusion.2
  473.6 8.1 %while.17 = (s32[]{:T(128)}, f32[1,512,512]{2,1,0:T(8,128)S(1)}, s32[4,2]{0,1:T(2,128)S(1)}, f32[4,1,128,128]{3,2,1,0:T(8,128)S(1)}, s32[]{:T(128)}) while((s32[]{:T(128)}, f32[1,512,512]{2,1,0:T(8,128)S(1)}, s32[4,2]{0,1:T(2,128)S(1)}, f32[4,1,128,128]{3,2,1,0:T(8,128)S(1)}, s32[]{:T(128)}) %tuple.68), condition=%wide.while_cond, body=%wide.while_body.sunk | while | flops 2 | bytes 131181 | solution.py:54
  473.7 0.6 fusion.74
  474.3 1.3 bitcast_dynamic-update-slice_fusion.10
  475.7 0.6 fusion.74
  476.3 1.3 bitcast_dynamic-update-slice_fusion.10
  477.7 0.6 fusion.74
  478.4 1.3 bitcast_dynamic-update-slice_fusion.10
  479.8 0.6 fusion.74
  480.4 1.3 bitcast_dynamic-update-slice_fusion.10
  481.7 39.3 %custom-call.41 = f32[1,4,128,128]{2,3,1,0:T(8,128)S(1)} custom-call(f32[1,4,128,128]{3,2,1,0:T(8,128)S(1)} %bitcast.228), custom_call_target="InvertDiagBlocksLowerTriangular" | custom-call | tf_op jit(solution)/shard_map/triangular_solve | solution.py:54
  521.1 0.3 bitcast_convert_fusion
  521.4 0.4 fusion.38
  521.8 0.3 fusion.64
  522.1 0.6 fusion.41
  522.7 0.3 fusion.63
  523.0 0.8 fusion.43
  523.9 0.3 fusion.44
  524.2 0.7 pad_maximum_fusion
  525.0 27.2 %all-gather.2.cloned.1.call-done = bf16[1,2048,512]{1,2,0:T(8,128)(2,1)} async-done(((bf16[1,256,512]{1,2,0:T(8,128)(2,1)}), bf16[1,2048,512]{1,2,0:T(8,128)(2,1)}) %all-gather.2.cloned.1.call-update) | async-done | bytes 2097168 | tf_op jit(solution)/shard_map/all_gather | solution.py:59
  552.1 13.6 %fusion.31 = f32[512,1,3584]{2,0,1:T(8,128)} fusion(bf16[1,2048,3584]{2,1,0:T(8,128)(2,1)} %param.4, bf16[1,2048,512]{1,2,0:T(8,128)(2,1)} %all-gather.2.cloned.1.call-done), kind=kOutput, calls=%fused_computation.27 | convolution fusion | flops 7516192768 | bytes 24117248 | tf_op jit(solution)/shard_map/mdr,mdc->rmc/dot_general | solution.py:57
  565.7 127.9 %reduce-scatter.2.cloned.1.call-done = f32[128,1,3584]{2,0,1:T(8,128)} async-done(((f32[512,1,3584]{2,0,1:T(8,128)}), f32[128,1,3584]{2,0,1:T(8,128)}) %reduce-scatter.2.cloned.1.call-update) | async-done | bytes 1835024 | tf_op jit(solution)/shard_map/reduce_scatter | solution.py:63
  693.6 2.5 convert_element_type.66
  (30 shorter events, 0.9 us)
Async XLA Ops:
  29.6 167.7 %all-to-all-start = ((bf16[8,1,256,3584]{3,2,1,0:T(8,128)(2,1)}), bf16[8,1,256,3584]{3,2,1,0:T(8,128)(2,1)}, u32[]{:S(2)}, u32[]{:S(2)}) async-start(bf16[8,1,256,3584]{3,2,1,0:T(8,128)(2,1)} %bitcast_dynamic-update-slice_fusion.1), calls=%async_computation | async-start | bytes 29360128 | tf_op jit(solution)/shard_map/all_to_all | solution.py:28
  35.1 351.9 %all-reduce.3.cloned.1.call-start = ((), (), s32[]{:S(2)}) async-start(), calls=%async_computation.2 | async-start | bytes 2097152 | tf_op jit(solution)/shard_map/psum | solution.py:51
  255.8 296.3 %all-gather.2.cloned.1.call-start = ((), (), s32[]{:S(2)}) async-start(), calls=%async_computation.3 | async-start | bytes 2359296 | tf_op jit(solution)/shard_map/all_gather | solution.py:59
  524.9 168.7 %reduce-scatter.2.cloned.1.call-start = ((), (), s32[]{:S(2)}) async-start(), calls=%async_computation.4 | async-start | bytes 9175040 | tf_op jit(solution)/shard_map/reduce_scatter | solution.py:63
Sparse Core Ops, SparseCore 0:
  256.0 130.9 all-reduce.2
  525.0 27.0 all-gather.1
  565.8 127.7 reduce-scatter.1
